TPU v7x, 256 devices: a whole 4x4x8 slice. The times are simulated.
256 devices in a mesh: mem: 4 (over x), col: 64 (over y, z, core).
Axes of the slice: x: 4, y: 4, z: 8, core: 2. Of those that a mesh axis runs over, the one named last changes fastest.
Arguments:
- perturbations: bfloat16 [32, 256, 256, 128], P('mem', 'col'), may hold values from -4 to 4
- static_root: float32 [128, 128], replicated, may hold values from -0.5 to 1.5
- obs_jacobian: float32 [128, 128], replicated, may hold values from -0.5 to 0.5
- innovations: float32 [16384, 128], P('col'), may hold values from -6 to 6
- obs_weights: float32 [128], replicated, may hold values from 0.2 to 2
- length_scale: float32 [256, 256], P('col'), may hold values from 0.05 to 0.24
- obs_owner: int32 [16384, 1], P('col'), may hold values from 0 to 63; in each aligned block of 256 rows (0 to 255, 256 to 511, ...) at most 8 rows name the same one
- obs_cell: int32 [16384], P('col'), may hold values from 0 to 1023
- obs_count: int32 [64], P('col'), may hold values from 128 to 256, as said below
Outputs:
- increment: float32 [256, 256, 128], P('col', 'mem')
- control_static: float32 [256, 256, 128], P('col', 'mem')
- control_ensemble: float32 [32, 256, 256], P('mem', 'col')
Inputs may be any that keep to these rules, and one draw needn't show every extreme that they name: `obs_owner`: each holder's 256 rows name any one column block at most 8 times. `obs_count`: rows at or past a holder's count are padding and are ignored; at least one holder is full. `obs_cell`: the column within the owner's block, numbered y * 256 + x, where y is its grid row within the block (0 to 3).
All inputs are finite; a program needn't handle non-finite values.
Results may differ from a plain program's by a relative error of at most 0.004.
Values may be sent and summed in bfloat16 or wider, within the bound.
No kernel may reach another device: no remote copies, remote signals or barrier semaphores. Data moves between devices by JAX's collectives and lax.ppermute only.
A program may use at most 64 MiB of HBM per device.

v0:
```python
import jax
import jax.numpy as jnp
from jax import lax
from jax.sharding import PartitionSpec as P

NSWEEP = 4
ITERS = 2


def extended(block, sides, width):
    for axis, dim in sides:
        count = lax.axis_size(axis)
        forward = [(i, i + 1) for i in range(count - 1)]
        backward = [(target, source) for source, target in forward]
        low = lax.ppermute(
            lax.slice_in_dim(block, block.shape[dim] - width, None, axis=dim), axis, forward
        )
        high = lax.ppermute(lax.slice_in_dim(block, 0, width, axis=dim), axis, backward)
        block = jnp.concatenate([low, block, high], axis=dim)
    return block


def face_coefficients(length_scale):
    rimmed = extended(length_scale, (("col", 0),), 1)
    padded = jnp.pad(rimmed, ((0, 0), (1, 1)))
    return (
        jnp.sqrt(length_scale * padded[:-2, 1:-1]),
        jnp.sqrt(length_scale * padded[2:, 1:-1]),
        jnp.sqrt(length_scale * padded[1:-1, :-2]),
        jnp.sqrt(length_scale * padded[1:-1, 2:]),
    )


def sweeps(values, coeffs):
    face_up, face_down, face_left, face_right = coeffs
    for sweep_step in range(NSWEEP):
        rimmed = extended(values, (("col", 1),), 1)
        padded = jnp.pad(rimmed, ((0, 0), (0, 0), (1, 1)))
        centre = values
        values = (
            centre
            + face_up * (padded[:, :-2, 1:-1] - centre)
            + face_down * (padded[:, 2:, 1:-1] - centre)
            + face_left * (padded[:, 1:-1, :-2] - centre)
            + face_right * (padded[:, 1:-1, 2:] - centre)
        )
    return values


def local_inner(first, second):
    return jnp.sum(first[0] * second[0]) + jnp.sum(first[1] * second[1])


def shards(
    perturbations,
    static_root,
    obs_jacobian,
    innovations,
    obs_weights,
    length_scale,
    obs_owner,
    obs_cell,
    obs_count,
):
    members, rows_here, columns, features = perturbations.shape
    quarter = columns // lax.axis_size("mem")
    offset = lax.axis_index("mem") * quarter
    blocks = lax.axis_size("col")
    obs_dev, channels = innovations.shape
    capacity = max(2, 2 * obs_dev // blocks)
    total_slots = blocks * capacity
    coeffs = face_coefficients(length_scale)
    is_live = jnp.arange(obs_dev, dtype=jnp.int32) < obs_count[0]
    owner_ids = obs_owner[:, 0]
    onehot = (
        (owner_ids[:, None] == jnp.arange(blocks, dtype=jnp.int32)[None, :]) & is_live[:, None]
    ).astype(jnp.int32)
    slot_rank = jnp.sum((jnp.cumsum(onehot, axis=0) - onehot) * onehot, axis=1)
    slot_ids = jnp.where(is_live, owner_ids * capacity + slot_rank, total_slots)
    send_values = (
        jnp.zeros((total_slots, channels), jnp.float32).at[slot_ids].set(innovations, mode="drop")
    )
    send_cells = jnp.zeros((total_slots,), jnp.int32).at[slot_ids].set(obs_cell, mode="drop")
    send_marks = jnp.zeros((total_slots,), jnp.float32).at[slot_ids].set(1.0, mode="drop")
    got_values, got_cells, got_marks = (
        lax.all_to_all(
            send_values.reshape(blocks, capacity, channels),
            "col",
            split_axis=0,
            concat_axis=0,
            tiled=True,
        ),
        lax.all_to_all(
            send_cells.reshape(blocks, capacity), "col", split_axis=0, concat_axis=0, tiled=True
        ),
        lax.all_to_all(
            send_marks.reshape(blocks, capacity), "col", split_axis=0, concat_axis=0, tiled=True
        ),
    )
    got_values = got_values.reshape(total_slots, channels)
    got_cells = got_cells.reshape(total_slots)
    got_marks = got_marks.reshape(total_slots)
    obs_index = got_cells
    obs_gain = got_marks[:, None] * obs_weights[None, :]

    def spread_back(weighted):
        back = jnp.dot(weighted, obs_jacobian.T, precision=lax.Precision.HIGHEST)
        grid = jnp.zeros((rows_here * columns, features), jnp.float32).at[obs_index].add(back)
        return grid.reshape(rows_here, columns, features)

    def adjoint_map(gradient):
        own_gradient = lax.dynamic_slice_in_dim(gradient, offset, quarter, 1)
        rounded = gradient.astype(jnp.bfloat16)
        static = jnp.dot(
            own_gradient.reshape(rows_here * quarter, features),
            static_root.T,
            precision=lax.Precision.HIGHEST,
        ).reshape(rows_here, quarter, features)
        projected = jnp.einsum(
            "kyxf,yxf->kyx", perturbations, rounded, preferred_element_type=jnp.float32
        )
        return (static, sweeps(projected, coeffs))

    residual = adjoint_map(spread_back(obs_gain * got_values))
    direction = residual
    state = (jnp.zeros_like(residual[0]), jnp.zeros_like(residual[1]))
    increment = jnp.zeros((rows_here, quarter, features), jnp.float32)
    norm_now = lax.psum(local_inner(residual, residual), ("mem", "col"))
    for iteration in range(ITERS):
        smoothed = sweeps(direction[1], coeffs).astype(jnp.bfloat16)
        partial_sum = jnp.einsum(
            "kyxf,kyx->yxf", perturbations, smoothed, preferred_element_type=jnp.float32
        )
        forward_static = jnp.dot(
            direction[0].reshape(rows_here * quarter, features),
            static_root,
            precision=lax.Precision.HIGHEST,
        ).reshape(rows_here, quarter, features)
        own_slice = lax.dynamic_slice_in_dim(partial_sum, offset, quarter, 1) + forward_static
        partial_sum = lax.dynamic_update_slice_in_dim(partial_sum, own_slice, offset, 1)
        image_part = lax.psum(partial_sum, "mem")
        own_image = lax.dynamic_slice_in_dim(image_part, offset, quarter, 1)
        image_part, own_image = (image_part, own_image)
        gathered = image_part.reshape(rows_here * columns, features)[obs_index]
        model_obs = jnp.dot(gathered, obs_jacobian, precision=lax.Precision.HIGHEST)
        adj_static, adj_ensemble = adjoint_map(spread_back(obs_gain * model_obs))
        image = (direction[0] + adj_static, direction[1] + adj_ensemble)
        step = norm_now / lax.psum(local_inner(direction, image), ("mem", "col"))
        residual = (residual[0] - step * image[0], residual[1] - step * image[1])
        norm_next = lax.psum(local_inner(residual, residual), ("mem", "col"))
        state = (state[0] + step * direction[0], state[1] + step * direction[1])
        increment = increment + step * own_image
        ratio = norm_next / norm_now
        direction = (residual[0] + ratio * direction[0], residual[1] + ratio * direction[1])
        norm_now = norm_next
    return (increment, state[0], state[1])


def solution(mesh):
    placed = (
        P("mem", "col", None, None),
        P(),
        P(),
        P("col", None),
        P(),
        P("col", None),
        P("col", None),
        P("col"),
        P("col"),
    )
    return jax.shard_map(
        shards,
        mesh=mesh,
        in_specs=placed,
        out_specs=(P("col", "mem", None), P("col", "mem", None), P("mem", "col", None)),
        check_vma=False,
    )
```

profile of v0, /device:TPU:1, one launch (start us, length us, event | category | flops | bytes accessed | tf_op | source)
XLA Modules:
  0.0 626.9 jit_solution(7078985824332760388)
XLA Ops:
  13.3 13.1 %all-to-all-start = ((s32[64,1,8]{2,1,0:T(1,128)}), s32[64,1,8]{2,1,0:T(1,128)S(1)}, u32[]{:S(2)}, u32[]{:S(2)}) async-start(s32[64,1,8]{2,1,0:T(1,128)} %bitcast.6), calls=%async_computation | async-start | bytes 65536 | tf_op jit(solution)/shard_map/all_to_all | solution.py:93
  28.5 7.1 %all-to-all-done = s32[64,1,8]{2,1,0:T(1,128)S(1)} async-done(((s32[64,1,8]{2,1,0:T(1,128)}), s32[64,1,8]{2,1,0:T(1,128)S(1)}, u32[]{:S(2)}, u32[]{:S(2)}) %all-to-all-start) | async-done | bytes 2080 | tf_op jit(solution)/shard_map/all_to_all | solution.py:93
  35.7 4.7 all-to-all-start.1
  42.5 7.2 %all-to-all-done.1 = f32[64,1,8]{2,1,0:T(1,128)S(1)} async-done(((f32[64,1,8]{2,1,0:T(1,128)}), f32[64,1,8]{2,1,0:T(1,128)S(1)}, u32[]{:S(2)}, u32[]{:S(2)}) %all-to-all-start.1) | async-done | bytes 2080 | tf_op jit(solution)/shard_map/all_to_all | solution.py:96
  49.7 4.7 all-to-all-start.2
  55.3 3.5 collective-permute-start
  60.7 3.2 collective-permute-done.2
  73.1 3.3 collective-permute-start.1
  78.4 2.9 collective-permute-done.3
  100.7 4.8 collective-permute-done.9
  110.3 3.8 collective-permute-done.11
  118.7 3.8 collective-permute-done.13
  142.6 54.8 %all-reduce.25.cloned.1.call-done = f32[4,256,128]{2,1,0:T(8,128)} async-done(((f32[4,256,128]{2,1,0:T(8,128)}), f32[4,256,128]{2,1,0:T(8,128)}) %all-reduce.25.cloned.1.call-update) | async-done | bytes 524304 | tf_op jit(solution)/shard_map/psum | solution.py:141
  206.3 6.9 %collective-permute-start.18 = (f32[8,1,256]{2,1,0:T(1,128)S(1)}, f32[8,1,256]{2,1,0:T(1,128)S(1)}, u32[]{:S(2)}, u32[]{:S(2)}) collective-permute-start(f32[8,1,256]{2,1,0:T(1,128)S(1)} %get-tuple-element.30), channel_id=1, source_target_pairs={{0,1},{1,2},{2,3},{3,4},{4,5},{5,6},{6,7},{7,8},{8,9},{9,10},{10,1... | collective-permute-start | bytes 24584 | tf_op jit(solution)/shard_map/ppermute | solution.py:15
  215.1 3.0 collective-permute-done.19
  238.0 3.9 collective-permute-done.25
  245.4 80.6 %all-reduce.21 = (f32[]{:T(128)}, f32[]{:T(128)}) all-reduce(f32[]{:T(128)S(6)} %add.401, f32[]{:T(128)S(6)} %add.437), channel_id=1, replica_groups=mesh['mem'=4,'col'=64] {'mem','col'}, use_global_device_ids=true, to_apply=%region_9.10 | all-reduce | flops 2 | bytes 16 | tf_op jit(solution)/shard_map/psum | solution.py:128
  329.9 73.2 %psum.45 = f32[]{:T(128)} all-reduce(f32[]{:T(128)S(6)} %add.438), channel_id=1, replica_groups=mesh['mem'=4,'col'=64] {'mem','col'}, use_global_device_ids=true, to_apply=%region_17.18 | all-reduce | flops 1 | bytes 8 | tf_op jit(solution)/shard_map/psum | solution.py:150
  404.4 4.2 collective-permute-start.26
  440.4 48.7 %all-reduce.27.cloned.1.call-done = f32[4,256,128]{2,1,0:T(8,128)} async-done(((f32[4,256,128]{2,1,0:T(8,128)}), f32[4,256,128]{2,1,0:T(8,128)}) %all-reduce.27.cloned.1.call-update) | async-done | bytes 524304 | tf_op jit(solution)/shard_map/psum | solution.py:141
  498.1 6.8 %collective-permute-start.34 = (f32[8,1,256]{2,1,0:T(1,128)S(1)}, f32[8,1,256]{2,1,0:T(1,128)S(1)}, u32[]{:S(2)}, u32[]{:S(2)}) collective-permute-start(f32[8,1,256]{2,1,0:T(1,128)S(1)} %get-tuple-element.14), channel_id=1, source_target_pairs={{0,1},{1,2},{2,3},{3,4},{4,5},{5,6},{6,7},{7,8},{8,9},{9,10},{10,1... | collective-permute-start | bytes 24584 | tf_op jit(solution)/shard_map/ppermute | solution.py:15
  506.9 3.0 collective-permute-done.35
  529.8 4.0 collective-permute-done.41
  535.9 80.6 %psum.47 = f32[]{:T(128)} all-reduce(f32[]{:T(128)S(6)} %add.476), channel_id=1, replica_groups=mesh['mem'=4,'col'=64] {'mem','col'}, use_global_device_ids=true, to_apply=%region_22.23 | all-reduce | flops 1 | bytes 8 | tf_op jit(solution)/shard_map/psum | solution.py:148
  (212 shorter events, 169.8 us)
Async XLA Ops:
  13.3 22.4 %all-to-all-start = ((s32[64,1,8]{2,1,0:T(1,128)}), s32[64,1,8]{2,1,0:T(1,128)S(1)}, u32[]{:S(2)}, u32[]{:S(2)}) async-start(s32[64,1,8]{2,1,0:T(1,128)} %bitcast.6), calls=%async_computation | async-start | bytes 65536 | tf_op jit(solution)/shard_map/all_to_all | solution.py:93
  35.7 14.1 %all-to-all-start.1 = ((f32[64,1,8]{2,1,0:T(1,128)}), f32[64,1,8]{2,1,0:T(1,128)S(1)}, u32[]{:S(2)}, u32[]{:S(2)}) async-start(f32[64,1,8]{2,1,0:T(1,128)} %bitcast.8), calls=%async_computation.1 | async-start | bytes 65536 | tf_op jit(solution)/shard_map/all_to_all | solution.py:96
  49.7 17.7 %all-to-all-start.2 = ((f32[64,8,128]{2,1,0:T(8,128)}), f32[64,8,128]{2,1,0:T(8,128)S(1)}, u32[]{:S(2)}, u32[]{:S(2)}) async-start(f32[64,8,128]{2,1,0:T(8,128)} %bitcast.9), calls=%async_computation.2 | async-start | bytes 524288 | tf_op jit(solution)/shard_map/all_to_all | solution.py:86
  54.4 142.9 %all-reduce.25.cloned.1.call-start = ((), (), s32[]{:S(2)}) async-start(), calls=%async_computation.3 | async-start | bytes 1048576 | tf_op jit(solution)/shard_map/psum | solution.py:141
  55.3 5.5 collective-permute-start
  58.8 5.2 collective-permute-start.2
  73.1 5.3 collective-permute-start.1
  76.4 5.0 collective-permute-start.3
  90.8 5.2 collective-permute-start.7
  98.3 7.2 %collective-permute-start.9 = (f32[8,1,256]{2,1,0:T(1,128)S(1)}, f32[8,1,256]{2,1,0:T(1,128)S(1)}, u32[]{:S(2)}, u32[]{:S(2)}) collective-permute-start(f32[8,1,256]{2,1,0:T(1,128)S(1)} %get-tuple-element.41), channel_id=1, source_target_pairs={{1,0},{2,1},{3,2},{4,3},{5,4},{6,5},{7,6},{8,7},{9,8},{10,9},{11,1... | collective-permute-start | bytes 24584 | tf_op jit(solution)/shard_map/ppermute | solution.py:18
  107.9 6.2 collective-permute-start.11
  116.3 6.2 collective-permute-start.13
  122.7 5.2 collective-permute-start.14
  124.7 6.2 collective-permute-start.15
  131.1 5.3 collective-permute-start.16
  133.1 6.2 collective-permute-start.17
  142.5 346.6 %all-reduce.27.cloned.1.call-start = ((), (), s32[]{:S(2)}) async-start(), calls=%async_computation.4 | async-start | bytes 1048576 | tf_op jit(solution)/shard_map/psum | solution.py:141
  206.3 8.8 %collective-permute-start.18 = (f32[8,1,256]{2,1,0:T(1,128)S(1)}, f32[8,1,256]{2,1,0:T(1,128)S(1)}, u32[]{:S(2)}, u32[]{:S(2)}) collective-permute-start(f32[8,1,256]{2,1,0:T(1,128)S(1)} %get-tuple-element.30), channel_id=1, source_target_pairs={{0,1},{1,2},{2,3},{3,4},{4,5},{5,6},{6,7},{7,8},{8,9},{9,10},{10,1... | collective-permute-start | bytes 24584 | tf_op jit(solution)/shard_map/ppermute | solution.py:15
  232.8 5.2 collective-permute-start.24
  234.8 7.2 %collective-permute-start.25 = (f32[8,1,256]{2,1,0:T(1,128)S(1)}, f32[8,1,256]{2,1,0:T(1,128)S(1)}, u32[]{:S(2)}, u32[]{:S(2)}) collective-permute-start(f32[8,1,256]{2,1,0:T(1,128)S(1)} %get-tuple-element.25), channel_id=1, source_target_pairs={{1,0},{2,1},{3,2},{4,3},{5,4},{6,5},{7,6},{8,7},{9,8},{10,9},{11,1... | collective-permute-start | bytes 24584 | tf_op jit(solution)/shard_map/ppermute | solution.py:18
  404.4 6.4 %collective-permute-start.26 = (f32[8,1,256]{2,1,0:T(1,128)S(1)}, f32[8,1,256]{2,1,0:T(1,128)S(1)}, u32[]{:S(2)}, u32[]{:S(2)}) collective-permute-start(f32[8,1,256]{2,1,0:T(1,128)S(1)} %get-tuple-element.22), channel_id=1, source_target_pairs={{0,1},{1,2},{2,3},{3,4},{4,5},{5,6},{6,7},{7,8},{8,9},{9,10},{10,1... | collective-permute-start | bytes 24584 | tf_op jit(solution)/shard_map/ppermute | solution.py:15
  498.1 8.8 %collective-permute-start.34 = (f32[8,1,256]{2,1,0:T(1,128)S(1)}, f32[8,1,256]{2,1,0:T(1,128)S(1)}, u32[]{:S(2)}, u32[]{:S(2)}) collective-permute-start(f32[8,1,256]{2,1,0:T(1,128)S(1)} %get-tuple-element.14), channel_id=1, source_target_pairs={{0,1},{1,2},{2,3},{3,4},{4,5},{5,6},{6,7},{7,8},{8,9},{9,10},{10,1... | collective-permute-start | bytes 24584 | tf_op jit(solution)/shard_map/ppermute | solution.py:15
  524.6 5.2 collective-permute-start.40
  526.5 7.2 %collective-permute-start.41 = (f32[8,1,256]{2,1,0:T(1,128)S(1)}, f32[8,1,256]{2,1,0:T(1,128)S(1)}, u32[]{:S(2)}, u32[]{:S(2)}) collective-permute-start(f32[8,1,256]{2,1,0:T(1,128)S(1)} %get-tuple-element.9), channel_id=1, source_target_pairs={{1,0},{2,1},{3,2},{4,3},{5,4},{6,5},{7,6},{8,7},{9,8},{10,9},{11,1... | collective-permute-start | bytes 24584 | tf_op jit(solution)/shard_map/ppermute | solution.py:18
  (31 other events, 351.4 us)
Sparse Core Ops, SparseCore 0:
  142.7 54.6 all-reduce.24
  440.6 48.5 all-reduce.26
where the time goes:
time: 629 us; the launch traced here: 627 us
  blocking collectives  234 us (37%)
  waiting for transfers between devices  182 us (29%)
  starting transfers between devices  127 us (20%)
  between operations  25.3 us (4%)
  other arithmetic  22.1 us (4%)
  local copies, waits for them, and re-layouts  18.9 us (3%)
  matrix products  17.4 us (3%)
    psum x2, waiting for transfers between devices, shards(): image_part = lax.psum(partial_sum, 'mem')  104 us
    psum x1, blocking collectives, shards(): norm_now = lax.psum(local_inner(residual, residual), ('mem', 'col'))  80.6 us
    psum x1, blocking collectives, shards(): step = norm_now / lax.psum(local_inner(direction, image), ('mem', 'col'))  80.6 us
    psum x1, blocking collectives, shards(): norm_next = lax.psum(local_inner(residual, residual), ('mem', 'col'))  73.2 us
    ppermute x21, waiting for transfers between devices, extended(): lax.ppermute(lax.slice_in_dim(block, 0, width, axis=dim), axis, backward)  64.5 us
    ppermute x21, starting transfers between devices, extended(): lax.ppermute(lax.slice_in_dim(block, block.shape[dim] - width, None, axis...  56 us
    ppermute x21, starting transfers between devices, extended(): lax.ppermute(lax.slice_in_dim(block, 0, width, axis=dim), axis, backward)  47.9 us
    all_to_all x1, starting transfers between devices, shards(): lax.all_to_all(send_cells.reshape(blocks, capacity), 'col', split_axis=0,...  13.1 us
  transfers between devices with their start and end apart: 47, of which 25 were waited for; matrix products, arithmetic and copies ran while one was open for 2% of the time, Pallas kernels for 0%

commit v1 on v0

--- a/solution.py
+++ b/solution.py
@@ -2,6 +2,7 @@
 import jax.numpy as jnp
 from jax import lax
 from jax.sharding import PartitionSpec as P
+from jax.lax import axis_size, ppermute
 
 NSWEEP = 4
 ITERS = 2
@@ -138,7 +139,13 @@
         ).reshape(rows_here, quarter, features)
         own_slice = lax.dynamic_slice_in_dim(partial_sum, offset, quarter, 1) + forward_static
         partial_sum = lax.dynamic_update_slice_in_dim(partial_sum, own_slice, offset, 1)
-        image_part = lax.psum(partial_sum, "mem")
+        n_dev_all = axis_size("mem")
+        image_part = partial_sum
+        for dev_i in [
+            [(idx, idx ^ s) for idx in range(n_dev_all)] for s in (1, 2, 4, 8, 16) if s < n_dev_all
+        ]:
+            w1 = ppermute(image_part, "mem", perm=dev_i)
+            image_part = image_part + w1
         own_image = lax.dynamic_slice_in_dim(image_part, offset, quarter, 1)
         image_part, own_image = (image_part, own_image)
         gathered = image_part.reshape(rows_here * columns, features)[obs_index]

time: 629 us -> 587 us (0.933); the launches traced: 627 us -> 576 us
  waiting for transfers between devices: 182 us -> 126 us
  between operations: 25.3 us -> 11.9 us
  blocking collectives: 234 us -> 245 us
    psum x2 -> x0, waiting for transfers between devices: 104 us -> none  [shards(): image_part = lax.psum(partial_sum, 'mem')]
    ppermute x0 -> x4, waiting for transfers between devices: none -> 47.1 us  [shards(): w1 = ppermute(image_part, 'mem', perm=dev_i)]
    ppermute x0 -> x4, starting transfers between devices: none -> 6.79 us  [shards(): w1 = ppermute(image_part, 'mem', perm=dev_i)]
  transfers between devices with their start and end apart: 47 -> 49, of which waited for: 25 -> 27; matrix products, arithmetic and copies ran while one was open for 2% -> 2% of each run, Pallas kernels for 0% -> 0%
where the time goes in v1:
time: 587 us; the launch traced here: 576 us
  blocking collectives  245 us (42%)
  starting transfers between devices  130 us (22%)
  waiting for transfers between devices  126 us (21%)
  other arithmetic  26.2 us (4%)
  matrix products  19.9 us (3%)
  local copies, waits for them, and re-layouts  17.5 us (3%)
  between operations  11.9 us (2%)
    psum x1, blocking collectives, shards(): norm_now = lax.psum(local_inner(residual, residual), ('mem', 'col'))  86.9 us
    psum x1, blocking collectives, shards(): step = norm_now / lax.psum(local_inner(direction, image), ('mem', 'col'))  85.1 us
    psum x1, blocking collectives, shards(): norm_next = lax.psum(local_inner(residual, residual), ('mem', 'col'))  72.8 us
    ppermute x21, waiting for transfers between devices, extended(): lax.ppermute(lax.slice_in_dim(block, 0, width, axis=dim), axis, backward)  64.6 us
    ppermute x21, starting transfers between devices, extended(): lax.ppermute(lax.slice_in_dim(block, block.shape[dim] - width, None, axis...  53 us
    ppermute x21, starting transfers between devices, extended(): lax.ppermute(lax.slice_in_dim(block, 0, width, axis=dim), axis, backward)  47.5 us
    ppermute x4, waiting for transfers between devices, shards(): w1 = ppermute(image_part, 'mem', perm=dev_i)  47.1 us
    all_to_all x1, starting transfers between devices, shards(): lax.all_to_all(send_cells.reshape(blocks, capacity), 'col', split_axis=0,...  13.1 us
  transfers between devices with their start and end apart: 49, of which 27 were waited for; matrix products, arithmetic and copies ran while one was open for 2% of the time, Pallas kernels for 0%

profile of v1, /device:TPU:1, one launch (start us, length us, event | category | flops | bytes accessed | tf_op | source)
XLA Modules:
  0.0 576.1 jit_solution(8875814908723273261)
XLA Ops:
  6.7 13.1 %all-to-all-start = ((s32[64,1,8]{2,1,0:T(1,128)}), s32[64,1,8]{2,1,0:T(1,128)S(1)}, u32[]{:S(2)}, u32[]{:S(2)}) async-start(s32[64,1,8]{2,1,0:T(1,128)} %bitcast.6), calls=%async_computation | async-start | bytes 65536 | tf_op jit(solution)/shard_map/all_to_all | solution.py:94
  22.0 7.1 %all-to-all-done = s32[64,1,8]{2,1,0:T(1,128)S(1)} async-done(((s32[64,1,8]{2,1,0:T(1,128)}), s32[64,1,8]{2,1,0:T(1,128)S(1)}, u32[]{:S(2)}, u32[]{:S(2)}) %all-to-all-start) | async-done | bytes 2080 | tf_op jit(solution)/shard_map/all_to_all | solution.py:94
  29.1 4.7 all-to-all-start.1
  36.0 7.2 %all-to-all-done.1 = f32[64,1,8]{2,1,0:T(1,128)S(1)} async-done(((f32[64,1,8]{2,1,0:T(1,128)}), f32[64,1,8]{2,1,0:T(1,128)S(1)}, u32[]{:S(2)}, u32[]{:S(2)}) %all-to-all-start.1) | async-done | bytes 2080 | tf_op jit(solution)/shard_map/all_to_all | solution.py:97
  43.2 4.7 all-to-all-start.2
  48.7 3.5 collective-permute-start
  66.5 3.3 collective-permute-start.1
  94.1 4.8 collective-permute-done.9
  103.7 3.6 collective-permute-done.11
  111.9 3.8 collective-permute-done.13
  129.0 3.5 collective-permute-done.17
  136.2 10.3 %collective-permute-done.18 = f32[4,256,128]{2,1,0:T(8,128)S(1)} collective-permute-done((f32[4,256,128]{2,1,0:T(8,128)S(1)}, f32[4,256,128]{2,1,0:T(8,128)S(1)}, u32[]{:S(2)}, u32[]{:S(2)}) %collective-permute-start.18) | collective-permute-done | bytes 524320 | tf_op jit(solution)/shard_map/ppermute | solution.py:147
  149.4 11.4 %collective-permute-done.19 = f32[4,256,128]{2,1,0:T(8,128)S(1)} collective-permute-done((f32[4,256,128]{2,1,0:T(8,128)S(1)}, f32[4,256,128]{2,1,0:T(8,128)S(1)}, u32[]{:S(2)}, u32[]{:S(2)}) %collective-permute-start.19) | collective-permute-done | bytes 524320 | tf_op jit(solution)/shard_map/ppermute | solution.py:147
  169.8 5.6 collective-permute-start.20
  192.5 4.2 collective-permute-done.25
  202.3 4.5 collective-permute-done.27
  210.2 86.9 %all-reduce.21 = (f32[]{:T(128)}, f32[]{:T(128)}) all-reduce(f32[]{:T(128)S(6)} %add.409, f32[]{:T(128)S(6)} %add.447), channel_id=1, replica_groups=mesh['mem'=4,'col'=64] {'mem','col'}, use_global_device_ids=true, to_apply=%region_9.10 | all-reduce | flops 2 | bytes 16 | tf_op jit(solution)/shard_map/psum | solution.py:129
  301.0 72.8 %psum.30 = f32[]{:T(128)} all-reduce(f32[]{:T(128)S(6)} %add.448), channel_id=1, replica_groups=mesh['mem'=4,'col'=64] {'mem','col'}, use_global_device_ids=true, to_apply=%region_16.17 | all-reduce | flops 1 | bytes 8 | tf_op jit(solution)/shard_map/psum | solution.py:157
  375.0 4.2 collective-permute-start.28
  410.9 11.7 %collective-permute-done.36 = f32[4,256,128]{2,1,0:T(8,128)S(1)} collective-permute-done((f32[4,256,128]{2,1,0:T(8,128)S(1)}, f32[4,256,128]{2,1,0:T(8,128)S(1)}, u32[]{:S(2)}, u32[]{:S(2)}) %collective-permute-start.36) | collective-permute-done | bytes 524320 | tf_op jit(solution)/shard_map/ppermute | solution.py:147
  424.4 13.7 %collective-permute-done.37 = f32[4,256,128]{2,1,0:T(8,128)S(1)} collective-permute-done((f32[4,256,128]{2,1,0:T(8,128)S(1)}, f32[4,256,128]{2,1,0:T(8,128)S(1)}, u32[]{:S(2)}, u32[]{:S(2)}) %collective-permute-start.37) | collective-permute-done | bytes 524320 | tf_op jit(solution)/shard_map/ppermute | solution.py:147
  443.2 3.5 scatter_custom_fusion.5
  452.8 4.9 collective-permute-start.38
  488.0 85.1 %psum.31 = f32[]{:T(128)} all-reduce(f32[]{:T(128)S(6)} %add.488), channel_id=1, replica_groups=mesh['mem'=4,'col'=64] {'mem','col'}, use_global_device_ids=true, to_apply=%region_20.21 | all-reduce | flops 1 | bytes 8 | tf_op jit(solution)/shard_map/psum | solution.py:155
  (218 shorter events, 186.1 us)
Async XLA Ops:
  6.7 22.4 %all-to-all-start = ((s32[64,1,8]{2,1,0:T(1,128)}), s32[64,1,8]{2,1,0:T(1,128)S(1)}, u32[]{:S(2)}, u32[]{:S(2)}) async-start(s32[64,1,8]{2,1,0:T(1,128)} %bitcast.6), calls=%async_computation | async-start | bytes 65536 | tf_op jit(solution)/shard_map/all_to_all | solution.py:94
  29.1 14.1 %all-to-all-start.1 = ((f32[64,1,8]{2,1,0:T(1,128)}), f32[64,1,8]{2,1,0:T(1,128)S(1)}, u32[]{:S(2)}, u32[]{:S(2)}) async-start(f32[64,1,8]{2,1,0:T(1,128)} %bitcast.8), calls=%async_computation.1 | async-start | bytes 65536 | tf_op jit(solution)/shard_map/all_to_all | solution.py:97
  43.2 17.7 %all-to-all-start.2 = ((f32[64,8,128]{2,1,0:T(8,128)}), f32[64,8,128]{2,1,0:T(8,128)S(1)}, u32[]{:S(2)}, u32[]{:S(2)}) async-start(f32[64,8,128]{2,1,0:T(8,128)} %bitcast.9), calls=%async_computation.2 | async-start | bytes 524288 | tf_op jit(solution)/shard_map/all_to_all | solution.py:87
  48.7 5.5 collective-permute-start
  66.5 5.3 collective-permute-start.1
  84.2 5.2 collective-permute-start.7
  91.7 7.2 %collective-permute-start.9 = (f32[8,1,256]{2,1,0:T(1,128)S(1)}, f32[8,1,256]{2,1,0:T(1,128)S(1)}, u32[]{:S(2)}, u32[]{:S(2)}) collective-permute-start(f32[8,1,256]{2,1,0:T(1,128)S(1)} %get-tuple-element.41), channel_id=1, source_target_pairs={{1,0},{2,1},{3,2},{4,3},{5,4},{6,5},{7,6},{8,7},{9,8},{10,9},{11,1... | collective-permute-start | bytes 24584 | tf_op jit(solution)/shard_map/ppermute | solution.py:19
  101.1 6.2 %collective-permute-start.11 = (f32[8,1,256]{2,1,0:T(1,128)S(1)}, f32[8,1,256]{2,1,0:T(1,128)S(1)}, u32[]{:S(2)}, u32[]{:S(2)}) collective-permute-start(f32[8,1,256]{2,1,0:T(1,128)S(1)} %get-tuple-element.39), channel_id=1, source_target_pairs={{1,0},{2,1},{3,2},{4,3},{5,4},{6,5},{7,6},{8,7},{9,8},{10,9},{11,1... | collective-permute-start | bytes 24584 | tf_op jit(solution)/shard_map/ppermute | solution.py:19
  109.5 6.2 %collective-permute-start.13 = (f32[8,1,256]{2,1,0:T(1,128)S(1)}, f32[8,1,256]{2,1,0:T(1,128)S(1)}, u32[]{:S(2)}, u32[]{:S(2)}) collective-permute-start(f32[8,1,256]{2,1,0:T(1,128)S(1)} %get-tuple-element.37), channel_id=1, source_target_pairs={{1,0},{2,1},{3,2},{4,3},{5,4},{6,5},{7,6},{8,7},{9,8},{10,9},{11,1... | collective-permute-start | bytes 24584 | tf_op jit(solution)/shard_map/ppermute | solution.py:19
  116.0 5.2 collective-permute-start.14
  117.9 6.2 %collective-permute-start.15 = (f32[8,1,256]{2,1,0:T(1,128)S(1)}, f32[8,1,256]{2,1,0:T(1,128)S(1)}, u32[]{:S(2)}, u32[]{:S(2)}) collective-permute-start(f32[8,1,256]{2,1,0:T(1,128)S(1)} %get-tuple-element.35), channel_id=1, source_target_pairs={{1,0},{2,1},{3,2},{4,3},{5,4},{6,5},{7,6},{8,7},{9,8},{10,9},{11,1... | collective-permute-start | bytes 24584 | tf_op jit(solution)/shard_map/ppermute | solution.py:19
  126.3 6.2 %collective-permute-start.17 = (f32[8,1,256]{2,1,0:T(1,128)S(1)}, f32[8,1,256]{2,1,0:T(1,128)S(1)}, u32[]{:S(2)}, u32[]{:S(2)}) collective-permute-start(f32[8,1,256]{2,1,0:T(1,128)S(1)} %get-tuple-element.33), channel_id=1, source_target_pairs={{1,0},{2,1},{3,2},{4,3},{5,4},{6,5},{7,6},{8,7},{9,8},{10,9},{11,1... | collective-permute-start | bytes 24584 | tf_op jit(solution)/shard_map/ppermute | solution.py:19
  134.9 11.6 %collective-permute-start.18 = (f32[4,256,128]{2,1,0:T(8,128)S(1)}, f32[4,256,128]{2,1,0:T(8,128)S(1)}, u32[]{:S(2)}, u32[]{:S(2)}) collective-permute-start(f32[4,256,128]{2,1,0:T(8,128)S(1)} %add_dynamic-update-slice_fusion), channel_id=1, source_target_pairs={{0,64},{64,0},{128,192},{192,128},{1,65},{65,1},{129,193},{193,129... | collective-permute-start | bytes 1572872 | tf_op jit(solution)/shard_map/ppermute | solution.py:147
  146.6 14.2 %collective-permute-start.19 = (f32[4,256,128]{2,1,0:T(8,128)S(1)}, f32[4,256,128]{2,1,0:T(8,128)S(1)}, u32[]{:S(2)}, u32[]{:S(2)}) collective-permute-start(f32[4,256,128]{2,1,0:T(8,128)S(1)} %add.427), channel_id=1, source_target_pairs={{0,128},{64,192},{128,0},{192,64},{1,129},{65,193},{129,1},{193,65... | collective-permute-start | bytes 1572872 | tf_op jit(solution)/shard_map/ppermute | solution.py:147
  169.8 7.5 %collective-permute-start.20 = (f32[8,1,256]{2,1,0:T(1,128)S(1)}, f32[8,1,256]{2,1,0:T(1,128)S(1)}, u32[]{:S(2)}, u32[]{:S(2)}) collective-permute-start(f32[8,1,256]{2,1,0:T(1,128)S(1)} %get-tuple-element.30), channel_id=1, source_target_pairs={{0,1},{1,2},{2,3},{3,4},{4,5},{5,6},{6,7},{7,8},{8,9},{9,10},{10,1... | collective-permute-start | bytes 24584 | tf_op jit(solution)/shard_map/ppermute | solution.py:16
  182.6 5.3 collective-permute-start.23
  190.5 6.3 %collective-permute-start.25 = (f32[8,1,256]{2,1,0:T(1,128)S(1)}, f32[8,1,256]{2,1,0:T(1,128)S(1)}, u32[]{:S(2)}, u32[]{:S(2)}) collective-permute-start(f32[8,1,256]{2,1,0:T(1,128)S(1)} %get-tuple-element.27), channel_id=1, source_target_pairs={{1,0},{2,1},{3,2},{4,3},{5,4},{6,5},{7,6},{8,7},{9,8},{10,9},{11,1... | collective-permute-start | bytes 24584 | tf_op jit(solution)/shard_map/ppermute | solution.py:19
  197.0 5.2 collective-permute-start.26
  199.0 7.8 %collective-permute-start.27 = (f32[8,1,256]{2,1,0:T(1,128)S(1)}, f32[8,1,256]{2,1,0:T(1,128)S(1)}, u32[]{:S(2)}, u32[]{:S(2)}) collective-permute-start(f32[8,1,256]{2,1,0:T(1,128)S(1)} %get-tuple-element.25), channel_id=1, source_target_pairs={{1,0},{2,1},{3,2},{4,3},{5,4},{6,5},{7,6},{8,7},{9,8},{10,9},{11,1... | collective-permute-start | bytes 24584 | tf_op jit(solution)/shard_map/ppermute | solution.py:19
  375.0 6.2 %collective-permute-start.28 = (f32[8,1,256]{2,1,0:T(1,128)S(1)}, f32[8,1,256]{2,1,0:T(1,128)S(1)}, u32[]{:S(2)}, u32[]{:S(2)}) collective-permute-start(f32[8,1,256]{2,1,0:T(1,128)S(1)} %get-tuple-element.22), channel_id=1, source_target_pairs={{0,1},{1,2},{2,3},{3,4},{4,5},{5,6},{6,7},{7,8},{8,9},{9,10},{10,1... | collective-permute-start | bytes 24584 | tf_op jit(solution)/shard_map/ppermute | solution.py:16
  409.9 12.8 %collective-permute-start.36 = (f32[4,256,128]{2,1,0:T(8,128)S(1)}, f32[4,256,128]{2,1,0:T(8,128)S(1)}, u32[]{:S(2)}, u32[]{:S(2)}) collective-permute-start(f32[4,256,128]{2,1,0:T(8,128)S(1)} %fusion.1), channel_id=1, source_target_pairs={{0,64},{64,0},{128,192},{192,128},{1,65},{65,1},{129,193},{193,129... | collective-permute-start | bytes 1572872 | tf_op jit(solution)/shard_map/ppermute | solution.py:147
  422.7 15.4 %collective-permute-start.37 = (f32[4,256,128]{2,1,0:T(8,128)S(1)}, f32[4,256,128]{2,1,0:T(8,128)S(1)}, u32[]{:S(2)}, u32[]{:S(2)}) collective-permute-start(f32[4,256,128]{2,1,0:T(8,128)S(1)} %add.468), channel_id=1, source_target_pairs={{0,128},{64,192},{128,0},{192,64},{1,129},{65,193},{129,1},{193,65... | collective-permute-start | bytes 1572872 | tf_op jit(solution)/shard_map/ppermute | solution.py:147
  452.8 6.9 %collective-permute-start.38 = (f32[8,1,256]{2,1,0:T(1,128)S(1)}, f32[8,1,256]{2,1,0:T(1,128)S(1)}, u32[]{:S(2)}, u32[]{:S(2)}) collective-permute-start(f32[8,1,256]{2,1,0:T(1,128)S(1)} %get-tuple-element.14), channel_id=1, source_target_pairs={{0,1},{1,2},{2,3},{3,4},{4,5},{5,6},{6,7},{7,8},{8,9},{9,10},{10,1... | collective-permute-start | bytes 24584 | tf_op jit(solution)/shard_map/ppermute | solution.py:16
  479.0 6.1 %collective-permute-start.44 = (f32[8,1,256]{2,1,0:T(1,128)S(1)}, f32[8,1,256]{2,1,0:T(1,128)S(1)}, u32[]{:S(2)}, u32[]{:S(2)}) collective-permute-start(f32[8,1,256]{2,1,0:T(1,128)S(1)} %get-tuple-element.8), channel_id=1, source_target_pairs={{0,1},{1,2},{2,3},{3,4},{4,5},{5,6},{6,7},{7,8},{8,9},{9,10},{10,1... | collective-permute-start | bytes 24584 | tf_op jit(solution)/shard_map/ppermute | solution.py:16
  (33 other events, 489.1 us)
